TPU v7x, 512 devices: a whole 4x4x16 slice. The times are simulated.
512 devices in a mesh: req: 16 (over z), tp: 32 (over x, y, core).
Axes of the slice: x: 4, y: 4, z: 16, core: 2. Of those that a mesh axis runs over, the one named last changes fastest.
Arguments:
- hidden: bfloat16 [1024, 5120], P(('req', 'tp')), may hold values from -6 to 6
- input_norm_gain: float32 [5120], replicated, may hold values from 0.1 to 1.9
- query_weight: bfloat16 [5120, 4096], P(None, 'tp'), may hold values from -1 to 1
- key_weight: bfloat16 [128, 8, 5120], P('tp'), may hold values from -0.078125 to 0.078125
- value_weight: bfloat16 [128, 8, 5120], P('tp'), may hold values from -0.078125 to 0.078125
- output_weight: bfloat16 [4096, 5120], P('tp'), may hold values from -0.09375 to 0.09375
- query_bias_vector: float32 [4096], P('tp'), may hold values from -3 to 3
- value_bias_vector: float32 [128, 8], P('tp'), may hold values from -3 to 3
- adapter_down_maps: bfloat16 [16, 5120, 32], P('req', 'tp'), may hold values from -0.078125 to 0.078125
- adapter_query_up: bfloat16 [16, 16, 4096], P('req', None, 'tp'), may hold values from -1.5 to 1.5
- adapter_value_up: bfloat16 [16, 16, 128, 8], P('req', None, 'tp'), may hold values from -1.5 to 1.5
- lengths: int32 [16, 8], P('req'), may hold values from 1 to 32, 64 in all within a row
- prompt_adapter: int32 [16, 8], P('req'), may hold values from 0 to 15
Outputs:
- output: bfloat16 [1024, 5120], P(('req', 'tp'))
All inputs are finite; a program needn't handle non-finite values.
Results may differ from a plain program's by a relative error of at most 0.019.
Values may be sent and summed in bfloat16 or wider, within the bound.
No kernel may reach another device: no remote copies, remote signals or barrier semaphores. Data moves between devices by JAX's collectives and lax.ppermute only.
A program may use at most 128 MiB of HBM per device.

v0:
```python
import jax
import jax.numpy as jnp
from jax import lax
from jax.sharding import PartitionSpec as P

HD = 128
HK = 8
HQ = 32
eps = 1e-06
rope_base = 1000000.0


def prompt_layout(prompt_length_list, group_tokens):
    count = prompt_length_list.shape[0]
    prompts = jnp.arange(count, dtype=jnp.int32)
    ends = jnp.sum(
        jnp.where(prompts[None, :] <= prompts[:, None], prompt_length_list[None, :], 0), axis=1
    )
    starts = ends - prompt_length_list
    places = jnp.arange(group_tokens, dtype=jnp.int32)
    group_entry = (places[:, None] >= starts[None, :]) & (places[:, None] < ends[None, :])
    segment = jnp.sum(jnp.where(group_entry, prompts[None, :], 0), axis=1)
    offset = places - jnp.sum(jnp.where(group_entry, starts[None, :], 0), axis=1)
    return (group_entry, segment, offset)


def rms_rows(source, input_norm_gain):
    values = source.astype(jnp.float32)
    return (
        values
        * lax.rsqrt(jnp.mean(values * values, axis=-1, keepdims=True) + eps)
        * input_norm_gain
    ).astype(jnp.bfloat16)


def rotate(values, offset):
    width = values.shape[-1]
    half_width = width // 2
    frequency = rope_base ** (-(jnp.arange(half_width, dtype=jnp.float32) * 2.0) / width)
    angles = offset.astype(jnp.float32)[:, None] * frequency[None, :]
    cosine = jnp.cos(angles)[:, None, :]
    sines = jnp.sin(angles)[:, None, :]
    lower_half = values[..., :half_width]
    upper_half = values[..., half_width:]
    return jnp.concatenate(
        [lower_half * cosine - upper_half * sines, upper_half * cosine + lower_half * sines],
        axis=-1,
    )


def rotate_rows(values_t, offset):
    width = values_t.shape[0]
    half_width = width // 2
    frequency = rope_base ** (-(jnp.arange(half_width, dtype=jnp.float32) * 2.0) / width)
    angles = offset.astype(jnp.float32)[None, :] * frequency[:, None]
    cosine = jnp.cos(angles)
    sines = jnp.sin(angles)
    lower_half = values_t[:half_width]
    upper_half = values_t[half_width:]
    return jnp.concatenate(
        [lower_half * cosine - upper_half * sines, upper_half * cosine + lower_half * sines], axis=0
    )


def attend(query_rot, key_rot_t, value_head_t, segment):
    scores = jnp.einsum(
        "qhd,dk->hqk", query_rot, key_rot_t, preferred_element_type=jnp.float32
    ) * HD ** (-0.5)
    places = jnp.arange(segment.shape[0], dtype=jnp.int32)
    allowed = (segment[:, None] == segment[None, :]) & (places[None, :] <= places[:, None])
    scores = jnp.where(allowed[None], scores, jnp.float32(-1e30))
    row_max = jnp.max(scores, axis=-1, keepdims=True)
    weights = jnp.exp(scores - row_max)
    probabilities = (weights / jnp.sum(weights, axis=-1, keepdims=True)).astype(jnp.bfloat16)
    mixed = jnp.einsum(
        "hqk,dk->qhd", probabilities, value_head_t, preferred_element_type=jnp.float32
    )
    return mixed.astype(jnp.bfloat16)


def shards(
    hidden,
    input_norm_gain,
    query_weight,
    key_weight,
    value_weight,
    output_weight,
    query_bias_vector,
    value_bias_vector,
    adapter_down_maps,
    adapter_query_up,
    adapter_value_up,
    lengths,
    prompt_adapter,
):
    tp_width = lax.axis_size("tp")
    tp_place = lax.axis_index("tp")
    tok_rows = hidden.shape[0]
    group_tokens = tok_rows * tp_width
    rank_extent = adapter_query_up.shape[1]
    entry_slice = key_weight.shape[0]
    kv_heads = key_weight.shape[1]
    feat_slice = adapter_down_maps.shape[1]
    head_count = query_weight.shape[1] // HD
    down_flat = adapter_down_maps.reshape(1, -1)
    query_flat = adapter_query_up.reshape(1, -1)
    value_flat = adapter_value_up.reshape(1, -1)
    bank_piece = jnp.concatenate([down_flat, query_flat, value_flat], axis=1)
    req_width = lax.axis_size("req")
    bank = lax.all_to_all(jnp.tile(bank_piece, (req_width, 1)), "req", 0, 0, tiled=True)
    adapter_total = bank.shape[0]
    n_down, n_query = (down_flat.shape[1], query_flat.shape[1])
    bank_down = bank[:, :n_down].reshape((adapter_total,) + adapter_down_maps.shape[1:])
    bank_query = bank[:, n_down : n_down + n_query].reshape(
        (adapter_total,) + adapter_query_up.shape[1:]
    )
    bank_value = bank[:, n_down + n_query :].reshape((adapter_total,) + adapter_value_up.shape[1:])
    prompt_length_list = lengths[0]
    adapter_choice_list = prompt_adapter[0]
    group_entry, segment, offset = prompt_layout(prompt_length_list, group_tokens)
    token_adapter = jnp.sum(jnp.where(group_entry, adapter_choice_list[None, :], 0), axis=1)
    adapter_pick = token_adapter[:, None] == jnp.arange(adapter_total, dtype=jnp.int32)[None, :]
    gathered = lax.all_gather(hidden, "tp", axis=0, tiled=True)
    normalized_input = rms_rows(gathered, input_norm_gain)
    own_features = lax.dynamic_slice_in_dim(normalized_input, tp_place * feat_slice, feat_slice, 1)
    terms = jnp.dot(
        own_features,
        jnp.transpose(bank_down, (1, 0, 2)).reshape(feat_slice, -1),
        preferred_element_type=jnp.float32,
    ).reshape(group_tokens, adapter_total, 2 * rank_extent)
    latent_part = jnp.sum(jnp.where(adapter_pick[:, :, None], terms, 0.0), axis=1)
    key_cols = jnp.einsum(
        "tm,ehm->het", normalized_input, key_weight, preferred_element_type=jnp.float32
    )
    value_cols = (
        jnp.einsum(
            "tm,ehm->het", normalized_input, value_weight, preferred_element_type=jnp.float32
        )
        + jnp.transpose(value_bias_vector)[:, :, None]
    )
    per_kv = tp_width // kv_heads
    key_send = jnp.repeat(key_cols, per_kv, axis=0).reshape(tp_width, -1)
    value_send = jnp.repeat(value_cols, per_kv, axis=0).reshape(tp_width, -1)
    latent_send = jnp.broadcast_to(latent_part.reshape(1, -1), (tp_width, latent_part.size))
    up_send = jnp.repeat(
        bank_value.transpose(3, 0, 1, 2).reshape(kv_heads, -1).astype(jnp.float32), per_kv, axis=0
    )
    n_key, n_value, n_latent = (key_send.shape[1], value_send.shape[1], latent_send.shape[1])
    kv_send = jnp.concatenate([key_send, value_send, latent_send, up_send], axis=1)
    kv_width = kv_send.shape[1]
    kv_pad = -kv_width % (8 * 128)
    kv_send = jnp.pad(kv_send, ((0, 0), (0, kv_pad))).reshape(tp_width, -1, 128)
    received = lax.all_to_all(kv_send, "tp", 0, 0, tiled=True).reshape(tp_width, -1)[:, :kv_width]
    key_head_t = received[:, :n_key].reshape(HD, group_tokens).astype(jnp.bfloat16)
    value_base_t = received[:, n_key : n_key + n_value].reshape(HD, group_tokens)
    latent = jnp.sum(
        received[:, n_key + n_value : n_key + n_value + n_latent].reshape(
            tp_width, group_tokens, 2 * rank_extent
        ),
        axis=0,
    ).astype(jnp.bfloat16)
    value_up_rows = received[:, n_key + n_value + n_latent :].reshape(
        tp_width, adapter_total * rank_extent, entry_slice
    )
    pick = adapter_pick.astype(jnp.bfloat16)
    query_latent = (latent[:, None, :rank_extent] * pick[:, :, None]).reshape(group_tokens, -1)
    value_latent = (latent[:, None, rank_extent:] * pick[:, :, None]).reshape(group_tokens, -1)
    query_rows = (
        jnp.dot(normalized_input, query_weight, preferred_element_type=jnp.float32)
        + query_bias_vector
        + jnp.dot(
            query_latent,
            bank_query.reshape(-1, bank_query.shape[-1]),
            preferred_element_type=jnp.float32,
        )
    )
    value_head_t = (
        value_base_t
        + jnp.einsum(
            "ta,sae->set",
            value_latent,
            value_up_rows.astype(jnp.bfloat16),
            preferred_element_type=jnp.float32,
        ).reshape(HD, group_tokens)
    ).astype(jnp.bfloat16)
    key_rot_t = rotate_rows(key_head_t.astype(jnp.float32), offset).astype(jnp.bfloat16)
    query_rot = rotate(query_rows.reshape(group_tokens, head_count, HD), offset).astype(
        jnp.bfloat16
    )
    mixed_heads = attend(query_rot, key_rot_t, value_head_t, segment).reshape(
        group_tokens, head_count * HD
    )
    block_terms = jnp.dot(mixed_heads, output_weight, preferred_element_type=jnp.float32).astype(
        jnp.bfloat16
    )
    owner_terms = lax.all_to_all(
        block_terms.reshape(tp_width, tok_rows, block_terms.shape[-1]), "tp", 0, 0, tiled=True
    )
    projected = jnp.sum(owner_terms.astype(jnp.float32), axis=0)
    return (hidden.astype(jnp.float32) + projected).astype(jnp.bfloat16)


def solution(mesh):
    return jax.shard_map(
        shards,
        mesh=mesh,
        in_specs=(
            P(("req", "tp"), None),
            P(),
            P(None, "tp"),
            P("tp", None, None),
            P("tp", None, None),
            P("tp", None),
            P("tp"),
            P("tp", None),
            P("req", "tp", None),
            P("req", None, "tp"),
            P("req", None, "tp", None),
            P("req", None),
            P("req", None),
        ),
        out_specs=P(("req", "tp"), None),
        check_vma=False,
    )
```

profile of v0, /device:TPU:1, one launch (start us, length us, event | category | flops | bytes accessed | tf_op | source)
XLA Modules:
  0.0 92.9 jit_solution(2929217116227379337)
XLA Ops:
  0.0 0.9 %copy.56 = bf16[1,160,32]{2,1,0:T(8,128)(2,1)S(1)} copy(bf16[1,160,32]{1,2,0:T(8,128)(2,1)} %param.21) | data formatting | bytes 20480 | tf_op args[8]
  1.0 0.1 reshape.350
  1.1 0.8 copy.57
  1.8 0.1 reshape.352
  1.9 0.7 copy.79
  2.6 0.1 maximum_reduce_fusion
  2.7 0.3 tile.2
  3.0 0.5 broadcast.220
  3.5 2.1 %reduce.5 = bf16[16,7680]{1,0:T(8,128)(2,1)S(1)} reduce(bf16[16,1,7680]{2,1,0:T(2,128)(2,1)S(1)} %tile.2, bf16[]{:T(256)} %broadcast.220), dimensions={1}, to_apply=%tile.2.reduce_sub_computation | reduce | bytes 491522 | tf_op jit(solution)/shard_map/tile | solution.py:110
  5.6 0.7 reshape.372
  6.3 15.7 %all-to-all-start = ((bf16[16,2,3840]{2,1,0:T(2,128)(2,1)}), bf16[16,2,3840]{2,1,0:T(2,128)(2,1)S(1)}, u32[]{:S(2)}, u32[]{:S(2)}) async-start(bf16[16,2,3840]{2,1,0:T(2,128)(2,1)} %reshape.372), calls=%async_computation | async-start | bytes 491520 | tf_op jit(solution)/shard_map/all_to_all | solution.py:110
  22.1 26.0 %all-gather = bf16[32,2,5120]{2,1,0:T(2,128)(2,1)S(1)} all-gather(bf16[1,2,5120]{2,1,0:T(2,128)(2,1)S(1)} %bitcast.107), channel_id=1, replica_groups=mesh['req'=16,'tp'=32] {'tp'}, dimensions={0}, use_global_device_ids=true | all-gather | bytes 675840 | tf_op jit(solution)/shard_map/all_gather | solution.py:123
  48.1 0.2 reshape.367
  48.3 0.0 copy-start.3
  48.3 0.2 multiply_reduce_fusion
  48.5 0.0 copy-start.4
  48.5 0.5 copy-done.3
  49.0 0.2 multiply_convert_fusion
  49.2 0.0 copy-start.7
  49.2 0.0 copy-start.6
  49.2 0.2 copy-done.1
  49.5 0.3 fusion.6
  49.8 0.1 reshape_reshape.10
  49.9 1.3 %convolution_bitcast_fusion.1 = f32[8,4,64]{2,0,1:T(8,128)S(1)} fusion(bf16[4,8,5120]{2,1,0:T(8,128)(2,1)} %param.16, bf16[64,5120]{1,0:T(8,128)(2,1)S(1)} %multiply_convert_fusion), kind=kOutput, calls=%fused_computation.18 | convolution fusion | flops 20971520 | bytes 991232 | tf_op jit(solution)/shard_map/tm,ehm->het/dot_general | solution.py:132
  51.2 0.1 reshape_reshape.9
  51.3 0.1 select_reduce_fusion.3
  51.4 0.1 select_reduce_fusion.1
  51.5 0.0 all-to-all-done
  51.5 0.2 reshape.373
  51.9 0.4 reshape.353
  52.3 0.3 copy.58
  52.6 0.3 fusion
  52.9 0.1 copy.59
  53.0 0.1 reshape.371
  53.1 0.1 copy.60
  53.2 0.6 copy.61
  53.8 0.2 copy.62
  54.2 0.0 copy-start.5
  54.2 0.9 copy.70
  55.1 5.1 %all-to-all-start.1 = ((f32[32,32,128]{2,1,0:T(8,128)}), f32[32,32,128]{2,1,0:T(8,128)S(1)}, u32[]{:S(2)}, u32[]{:S(2)}) async-start(f32[32,32,128]{2,1,0:T(8,128)} %bitcast.41), calls=%async_computation.1 | async-start | bytes 1048576 | tf_op jit(solution)/shard_map/all_to_all | solution.py:153
  60.2 1.7 %convolution_add_fusion.1 = f32[64,128]{1,0:T(8,128)S(1)} fusion(bf16[64,5120]{1,0:T(8,128)(2,1)S(1)} %multiply_convert_fusion, bf16[5120,128]{1,0:T(8,128)(2,1)} %param.15, f32[128]{0:T(128)S(1)} %copy-done.5), kind=kOutput, calls=%fused_computation.10 | convolution fusion | flops 83894272 | bytes 1999360 | tf_op jit(solution)/shard_map/dot_general | solution.py:169
  62.0 9.8 %all-to-all-done.1 = f32[32,32,128]{2,1,0:T(8,128)S(1)} async-done(((f32[32,32,128]{2,1,0:T(8,128)}), f32[32,32,128]{2,1,0:T(8,128)S(1)}, u32[]{:S(2)}, u32[]{:S(2)}) %all-to-all-start.1) | async-done | bytes 524320 | tf_op jit(solution)/shard_map/all_to_all | solution.py:153
  71.8 0.3 copy.77
  72.1 0.3 copy.80
  72.5 0.1 convert_element_type.96
  72.6 0.1 fusion.49
  72.7 0.1 copy.65
  72.8 0.1 copy.67
  72.8 0.1 slice.60
  72.9 0.1 slice.62
  73.0 0.2 copy.63
  73.2 0.2 copy.64
  73.4 0.1 reshape.358
  73.5 0.1 copy.66
  73.6 0.2 fusion.2
  73.7 0.2 fusion.41
  73.9 0.2 fusion.23
  74.2 0.2 fusion.50
  74.4 0.2 fusion.3
  74.6 0.5 convolution_convert_fusion
  75.2 0.2 reshape.362
  75.4 16.4 %all_to_all.19 = bf16[32,2,5120]{2,1,0:T(2,128)(2,1)S(1)} all-to-all(bf16[32,2,5120]{2,1,0:T(2,128)(2,1)S(1)} %reshape.362), channel_id=1, replica_groups=mesh['req'=16,'tp'=32] {'tp'}, dimensions={0} | all-to-all | bytes 1310720 | tf_op jit(solution)/shard_map/all_to_all | solution.py:196
  91.8 0.5 convert_reduce_fusion
  92.3 0.6 add_convert_fusion
  (36 shorter events, 0.5 us)
Async XLA Ops:
  0.0 74.6 %copy-start = (bf16[128,5120]{1,0:T(8,128)(2,1)S(1)}, bf16[128,5120]{1,0:T(8,128)(2,1)}, u32[]{:S(2)}) copy-start(bf16[128,5120]{1,0:T(8,128)(2,1)} %param.18) | copy-start | bytes 3932164
  0.0 22.1 %copy-start.2 = (bf16[2,5120]{1,0:T(2,128)(2,1)S(1)}, bf16[2,5120]{1,0:T(2,128)(2,1)}, u32[]{:S(2)}) copy-start(bf16[2,5120]{1,0:T(2,128)(2,1)} %param.13) | copy-start | bytes 61444
  6.3 45.2 %all-to-all-start = ((bf16[16,2,3840]{2,1,0:T(2,128)(2,1)}), bf16[16,2,3840]{2,1,0:T(2,128)(2,1)S(1)}, u32[]{:S(2)}, u32[]{:S(2)}) async-start(bf16[16,2,3840]{2,1,0:T(2,128)(2,1)} %reshape.372), calls=%async_computation | async-start | bytes 491520 | tf_op jit(solution)/shard_map/all_to_all | solution.py:110
  48.3 0.7 copy-start.3
  48.5 1.0 %copy-start.1 = (bf16[4,8,5120]{2,1,0:T(8,128)(2,1)S(1)}, bf16[4,8,5120]{2,1,0:T(8,128)(2,1)}, u32[]{:S(2)}) copy-start(bf16[4,8,5120]{2,1,0:T(8,128)(2,1)} %param.17) | copy-start | bytes 983044
  48.5 1.0 %copy-start.4 = (f32[4,8]{1,0:T(4,128)S(1)}, f32[4,8]{1,0:T(4,128)}, u32[]{:S(2)}) copy-start(f32[4,8]{1,0:T(4,128)} %param.20) | copy-start | bytes 388
  49.2 2.1 %copy-start.7 = (s32[1,8]{1,0:T(1,128)S(1)}, s32[1,8]{1,0:T(1,128)}, u32[]{:S(2)}) copy-start(s32[1,8]{1,0:T(1,128)} %param.24) | copy-start | bytes 100
  49.2 2.2 %copy-start.6 = (s32[1,8]{1,0:T(1,128)S(1)}, s32[1,8]{1,0:T(1,128)}, u32[]{:S(2)}) copy-start(s32[1,8]{1,0:T(1,128)} %param.25) | copy-start | bytes 100
  54.2 6.1 %copy-start.5 = (f32[128]{0:T(128)S(1)}, f32[128]{0:T(128)}, u32[]{:S(2)}) copy-start(f32[128]{0:T(128)} %param.19) | copy-start | bytes 1540
  55.1 16.7 %all-to-all-start.1 = ((f32[32,32,128]{2,1,0:T(8,128)}), f32[32,32,128]{2,1,0:T(8,128)S(1)}, u32[]{:S(2)}, u32[]{:S(2)}) async-start(f32[32,32,128]{2,1,0:T(8,128)} %bitcast.41), calls=%async_computation.1 | async-start | bytes 1048576 | tf_op jit(solution)/shard_map/all_to_all | solution.py:153
where the time goes:
time: 93.5 us; the launch traced here: 92.9 us
  blocking collectives  42.3 us (45%)
  starting transfers between devices  20.8 us (22%)
  local copies, waits for them, and re-layouts  10.3 us (11%)
  waiting for transfers between devices  9.85 us (11%)
  matrix products  4.66 us (5%)
  other arithmetic  4.52 us (5%)
    all_gather x1, blocking collectives, shards(): gathered = lax.all_gather(hidden, 'tp', axis=0, tiled=True)  26 us
    all_to_all x1, blocking collectives, shards(): lax.all_to_all(block_terms.reshape(tp_width, tok_rows, block_terms.shape[...  16.4 us
    all_to_all x1, starting transfers between devices, shards(): lax.all_to_all(jnp.tile(bank_piece, (req_width, 1)), 'req', 0, 0, tiled=T...  15.7 us
    all_to_all x1, waiting for transfers between devices, shards(): lax.all_to_all(kv_send, 'tp', 0, 0, tiled=True).reshape(tp_width, -1)  9.85 us
    unnamed x26, local copies, waits for them, and re-layouts  5.74 us
    all_to_all x1, starting transfers between devices, shards(): lax.all_to_all(kv_send, 'tp', 0, 0, tiled=True).reshape(tp_width, -1)  5.08 us
    another operation x1, other arithmetic, shards(): jnp.tile(bank_piece, (req_width, 1))  2.07 us
  transfers between devices with their start and end apart: 2, of which 1 were waited for; matrix products, arithmetic and copies ran while one was open for 5% of the time, Pallas kernels for 0%

commit v1 on v0

--- a/solution.py
+++ b/solution.py
@@ -2,6 +2,7 @@
 import jax.numpy as jnp
 from jax import lax
 from jax.sharding import PartitionSpec as P
+from jax.lax import all_to_all, axis_size
 
 HD = 128
 HK = 8
@@ -120,7 +121,15 @@
     group_entry, segment, offset = prompt_layout(prompt_length_list, group_tokens)
     token_adapter = jnp.sum(jnp.where(group_entry, adapter_choice_list[None, :], 0), axis=1)
     adapter_pick = token_adapter[:, None] == jnp.arange(adapter_total, dtype=jnp.int32)[None, :]
-    gathered = lax.all_gather(hidden, "tp", axis=0, tiled=True)
+    gathered = jnp.concatenate(
+        all_to_all(
+            jnp.stack([hidden] * axis_size("tp"), axis=0),
+            axis_name="tp",
+            split_axis=0,
+            concat_axis=0,
+        ),
+        axis=0,
+    )
     normalized_input = rms_rows(gathered, input_norm_gain)
     own_features = lax.dynamic_slice_in_dim(normalized_input, tp_place * feat_slice, feat_slice, 1)
     terms = jnp.dot(

time: 93.5 us -> 97.5 us (1.043)
  blocking collectives: 42.3 us -> 16.3 us
  waiting for transfers between devices: 9.85 us -> 28.3 us
  starting transfers between devices: 20.8 us -> 31.2 us
  other arithmetic: 4.52 us -> 5.66 us
    all_gather x1 -> x0, blocking collectives: 26 us -> none  [shards(): gathered = lax.all_gather(hidden, 'tp', axis=0, tiled=True)]
    all_to_all x0 -> x1, starting transfers between devices: none -> 10.4 us  [shards(): all_to_all(jnp.stack([hidden] * axis_size('tp'), axis=0), axis_name='tp',...]
    all_to_all x1, waiting for transfers between devices: 0.01 us -> 10.3 us  [shards(): lax.all_to_all(jnp.tile(bank_piece, (req_width, 1)), 'req', 0, 0, tiled=T...]
    all_to_all x0 -> x1, waiting for transfers between devices: none -> 8.04 us  [shards(): all_to_all(jnp.stack([hidden] * axis_size('tp'), axis=0), axis_name='tp',...]
    all_to_all x1, starting transfers between devices: 15.7 us -> 13 us  [shards(): lax.all_to_all(jnp.tile(bank_piece, (req_width, 1)), 'req', 0, 0, tiled=T...]
    all_to_all x1, starting transfers between devices: 5.08 us -> 7.81 us  [shards(): lax.all_to_all(kv_send, 'tp', 0, 0, tiled=True).reshape(tp_width, -1)]
    unnamed x26 -> x36, local copies, waits for them, and re-layouts: 5.74 us -> 3.57 us
    another operation x0 -> x1, local copies, waits for them, and re-layouts: none -> 2 us  [shards(): jnp.stack([hidden] * axis_size('tp'), axis=0)]
  transfers between devices with their start and end apart: 2 -> 3, of which waited for: 1 -> 3; matrix products, arithmetic and copies ran while one was open for 5% -> 10% of each run, Pallas kernels for 0% -> 0%
where the time goes in v1:
time: 97.5 us; the launch traced here: 97 us
  starting transfers between devices  31.2 us (32%)
  waiting for transfers between devices  28.3 us (29%)
  blocking collectives  16.3 us (17%)
  local copies, waits for them, and re-layouts  10.3 us (11%)
  other arithmetic  5.66 us (6%)
  matrix products  4.66 us (5%)
    all_to_all x1, blocking collectives, shards(): lax.all_to_all(block_terms.reshape(tp_width, tok_rows, block_terms.shape[...  16.3 us
    all_to_all x1, starting transfers between devices, shards(): lax.all_to_all(jnp.tile(bank_piece, (req_width, 1)), 'req', 0, 0, tiled=T...  13 us
    all_to_all x1, starting transfers between devices, shards(): all_to_all(jnp.stack([hidden] * axis_size('tp'), axis=0), axis_name='tp',...  10.4 us
    all_to_all x1, waiting for transfers between devices, shards(): lax.all_to_all(jnp.tile(bank_piece, (req_width, 1)), 'req', 0, 0, tiled=T...  10.3 us
    all_to_all x1, waiting for transfers between devices, shards(): lax.all_to_all(kv_send, 'tp', 0, 0, tiled=True).reshape(tp_width, -1)  9.95 us
    all_to_all x1, waiting for transfers between devices, shards(): all_to_all(jnp.stack([hidden] * axis_size('tp'), axis=0), axis_name='tp',...  8.04 us
    all_to_all x1, starting transfers between devices, shards(): lax.all_to_all(kv_send, 'tp', 0, 0, tiled=True).reshape(tp_width, -1)  7.81 us
    unnamed x36, local copies, waits for them, and re-layouts  3.57 us
  transfers between devices with their start and end apart: 3, of which 3 were waited for; matrix products, arithmetic and copies ran while one was open for 10% of the time, Pallas kernels for 0%

profile of v1, /device:TPU:1, one launch (start us, length us, event | category | flops | bytes accessed | tf_op | source)
XLA Modules:
  0.0 97.0 jit_solution(16961229776020003152)
XLA Ops:
  0.0 2.0 %stack.2 = bf16[32,2,5120]{2,1,0:T(2,128)(2,1)} broadcast(bf16[2,5120]{1,0:T(2,128)(2,1)} %param.13), dimensions={1,2} | broadcast | bytes 675840 | tf_op jit(solution)/shard_map/stack | solution.py:126
  2.0 10.4 %all-to-all-start = ((bf16[32,2,5120]{2,1,0:T(2,128)(2,1)}), bf16[32,2,5120]{2,1,0:T(2,128)(2,1)S(1)}, u32[]{:S(2)}, u32[]{:S(2)}) async-start(bf16[32,2,5120]{2,1,0:T(2,128)(2,1)} %stack.2), calls=%async_computation | async-start | bytes 1310720 | tf_op jit(solution)/shard_map/all_to_all | solution.py:125
  12.5 0.0 copy-start.12
  12.5 0.1 copy.56
  12.6 0.1 reshape.364
  12.7 0.1 copy.57
  12.8 0.1 reshape.366
  12.9 0.1 maximum_reduce_fusion
  13.0 0.3 tile.2
  13.3 0.5 broadcast.226
  13.8 2.1 %reduce.6 = bf16[16,7680]{1,0:T(8,128)(2,1)S(1)} reduce(bf16[16,1,7680]{2,1,0:T(2,128)(2,1)S(1)} %tile.2, bf16[]{:T(256)} %broadcast.226), dimensions={1}, to_apply=%tile.2.reduce_sub_computation | reduce | bytes 491522 | tf_op jit(solution)/shard_map/tile | solution.py:111
  15.9 0.8 reshape.384
  16.7 0.1 select_reduce_fusion.3
  16.8 0.7 select_reduce_fusion.1
  17.5 8.0 %all-to-all-done = bf16[32,2,5120]{2,1,0:T(2,128)(2,1)S(1)} async-done(((bf16[32,2,5120]{2,1,0:T(2,128)(2,1)}), bf16[32,2,5120]{2,1,0:T(2,128)(2,1)S(1)}, u32[]{:S(2)}, u32[]{:S(2)}) %all-to-all-start) | async-done | bytes 655392 | tf_op jit(solution)/shard_map/all_to_all | solution.py:125
  25.5 13.0 %all-to-all-start.1 = ((bf16[16,2,3840]{2,1,0:T(2,128)(2,1)}), bf16[16,2,3840]{2,1,0:T(2,128)(2,1)S(1)}, u32[]{:S(2)}, u32[]{:S(2)}) async-start(bf16[16,2,3840]{2,1,0:T(2,128)(2,1)} %reshape.384), calls=%async_computation.1 | async-start | bytes 491520 | tf_op jit(solution)/shard_map/all_to_all | solution.py:111
  38.5 0.8 multiply_reduce_fusion
  39.3 0.1 rsqrt.12
  39.4 0.2 reshape.377
  39.6 0.0 copy-start.1
  39.6 0.0 copy-start.7
  39.6 0.2 multiply_convert_fusion
  39.8 0.8 copy-done.1
  40.6 0.3 fusion.6
  40.9 0.1 reshape_reshape.10
  41.0 1.3 %convolution_bitcast_fusion.1 = f32[8,4,64]{2,0,1:T(8,128)S(1)} fusion(bf16[4,8,5120]{2,1,0:T(8,128)(2,1)} %param.16, bf16[64,5120]{1,0:T(8,128)(2,1)S(1)} %multiply_convert_fusion), kind=kOutput, calls=%fused_computation.18 | convolution fusion | flops 20971520 | bytes 991232 | tf_op jit(solution)/shard_map/tm,ehm->het/dot_general | solution.py:141
  42.3 0.1 reshape_reshape.9
  42.4 10.3 %all-to-all-done.1 = bf16[16,2,3840]{2,1,0:T(2,128)(2,1)S(1)} async-done(((bf16[16,2,3840]{2,1,0:T(2,128)(2,1)}), bf16[16,2,3840]{2,1,0:T(2,128)(2,1)S(1)}, u32[]{:S(2)}, u32[]{:S(2)}) %all-to-all-start.1) | async-done | bytes 245792 | tf_op jit(solution)/shard_map/all_to_all | solution.py:111
  52.7 0.2 reshape.385
  53.0 0.4 reshape.367
  53.5 0.3 copy.58
  53.8 0.3 fusion
  54.1 0.1 copy.59
  54.2 0.1 reshape.383
  54.3 0.1 copy.60
  54.4 0.6 copy.61
  55.0 0.2 copy.62
  55.4 0.9 copy.70
  56.3 7.8 %all-to-all-start.2 = ((f32[32,32,128]{2,1,0:T(8,128)}), f32[32,32,128]{2,1,0:T(8,128)S(1)}, u32[]{:S(2)}, u32[]{:S(2)}) async-start(f32[32,32,128]{2,1,0:T(8,128)} %bitcast.40), calls=%async_computation.2 | async-start | bytes 1048576 | tf_op jit(solution)/shard_map/all_to_all | solution.py:162
  64.2 1.7 %convolution_add_fusion.1 = f32[64,128]{1,0:T(8,128)S(1)} fusion(bf16[64,5120]{1,0:T(8,128)(2,1)S(1)} %multiply_convert_fusion, bf16[5120,128]{1,0:T(8,128)(2,1)} %param.15, f32[128]{0:T(128)S(1)} %copy-done.8), kind=kOutput, calls=%fused_computation.10 | convolution fusion | flops 83894272 | bytes 1999360 | tf_op jit(solution)/shard_map/dot_general | solution.py:178
  65.9 9.9 %all-to-all-done.2 = f32[32,32,128]{2,1,0:T(8,128)S(1)} async-done(((f32[32,32,128]{2,1,0:T(8,128)}), f32[32,32,128]{2,1,0:T(8,128)S(1)}, u32[]{:S(2)}, u32[]{:S(2)}) %all-to-all-start.2) | async-done | bytes 524320 | tf_op jit(solution)/shard_map/all_to_all | solution.py:162
  75.8 0.3 copy.77
  76.2 0.3 copy.80
  76.5 0.0 copy-start.10
  76.6 0.1 convert_element_type.104
  76.6 0.1 fusion.49
  76.7 0.1 copy.65
  76.8 0.1 copy.67
  76.9 0.1 slice.60
  77.0 0.1 slice.62
  77.0 0.2 copy.63
  77.2 0.2 copy.64
  77.4 0.1 reshape.372
  77.5 0.1 copy.66
  77.6 0.2 fusion.2
  77.8 0.2 fusion.41
  78.0 0.2 fusion.23
  78.2 0.2 fusion.50
  78.5 0.2 fusion.3
  78.7 0.5 convolution_convert_fusion
  79.2 0.2 reshape.376
  79.5 16.3 %all_to_all.24 = bf16[32,2,5120]{2,1,0:T(2,128)(2,1)S(1)} all-to-all(bf16[32,2,5120]{2,1,0:T(2,128)(2,1)S(1)} %reshape.376), channel_id=1, replica_groups=mesh['req'=16,'tp'=32] {'tp'}, dimensions={0} | all-to-all | bytes 1310720 | tf_op jit(solution)/shard_map/all_to_all | solution.py:205
  95.8 0.5 convert_reduce_fusion
  96.3 0.6 add_convert_fusion
  (49 shorter events, 0.5 us)
Async XLA Ops:
  0.0 78.7 %copy-start = (bf16[128,5120]{1,0:T(8,128)(2,1)S(1)}, bf16[128,5120]{1,0:T(8,128)(2,1)}, u32[]{:S(2)}) copy-start(bf16[128,5120]{1,0:T(8,128)(2,1)} %param.18) | copy-start | bytes 3932164
  0.0 12.5 %copy-start.4 = (bf16[1,160,32]{1,2,0:T(8,128)(2,1)S(1)}, bf16[1,160,32]{1,2,0:T(8,128)(2,1)}, u32[]{:S(2)}) copy-start(bf16[1,160,32]{1,2,0:T(8,128)(2,1)} %param.21) | copy-start | bytes 30724
  0.0 12.7 %copy-start.5 = (bf16[1,16,4,8]{1,3,2,0:T(8,128)(2,1)S(1)}, bf16[1,16,4,8]{1,3,2,0:T(8,128)(2,1)}, u32[]{:S(2)}) copy-start(bf16[1,16,4,8]{1,3,2,0:T(8,128)(2,1)} %param.23) | copy-start | bytes 3076
  0.0 12.9 %copy-start.6 = (bf16[1,16,128]{2,1,0:T(8,128)(2,1)S(1)}, bf16[1,16,128]{2,1,0:T(8,128)(2,1)}, u32[]{:S(2)}) copy-start(bf16[1,16,128]{2,1,0:T(8,128)(2,1)} %param.22) | copy-start | bytes 12292
  2.0 23.5 %all-to-all-start = ((bf16[32,2,5120]{2,1,0:T(2,128)(2,1)}), bf16[32,2,5120]{2,1,0:T(2,128)(2,1)S(1)}, u32[]{:S(2)}, u32[]{:S(2)}) async-start(bf16[32,2,5120]{2,1,0:T(2,128)(2,1)} %stack.2), calls=%async_computation | async-start | bytes 1310720 | tf_op jit(solution)/shard_map/all_to_all | solution.py:125
  12.5 4.2 %copy-start.12 = (s32[1,8]{1,0:T(1,128)S(1)}, s32[1,8]{1,0:T(1,128)}, u32[]{:S(2)}) copy-start(s32[1,8]{1,0:T(1,128)} %param.24) | copy-start | bytes 100
  12.5 4.3 %copy-start.9 = (s32[1,8]{1,0:T(1,128)S(1)}, s32[1,8]{1,0:T(1,128)}, u32[]{:S(2)}) copy-start(s32[1,8]{1,0:T(1,128)} %param.25) | copy-start | bytes 100
  25.5 27.2 %all-to-all-start.1 = ((bf16[16,2,3840]{2,1,0:T(2,128)(2,1)}), bf16[16,2,3840]{2,1,0:T(2,128)(2,1)S(1)}, u32[]{:S(2)}, u32[]{:S(2)}) async-start(bf16[16,2,3840]{2,1,0:T(2,128)(2,1)} %reshape.384), calls=%async_computation.1 | async-start | bytes 491520 | tf_op jit(solution)/shard_map/all_to_all | solution.py:111
  38.5 1.1 %copy-start.3 = (f32[5120]{0:T(1024)S(1)}, f32[5120]{0:T(1024)}, u32[]{:S(2)}) copy-start(f32[5120]{0:T(1024)} %param.14) | copy-start | bytes 61444
  39.6 1.0 %copy-start.1 = (bf16[4,8,5120]{2,1,0:T(8,128)(2,1)S(1)}, bf16[4,8,5120]{2,1,0:T(8,128)(2,1)}, u32[]{:S(2)}) copy-start(bf16[4,8,5120]{2,1,0:T(8,128)(2,1)} %param.17) | copy-start | bytes 983044
  39.6 1.0 copy-start.7
  55.3 8.8 %copy-start.11 = (s32[64]{0:T(128)S(1)}, s32[64]{0:T(128)}, u32[]{:S(2)}) copy-start(s32[64]{0:T(128)} %get-tuple-element.6) | copy-start | bytes 772
  55.4 8.8 %copy-start.8 = (f32[128]{0:T(128)S(1)}, f32[128]{0:T(128)}, u32[]{:S(2)}) copy-start(f32[128]{0:T(128)} %param.19) | copy-start | bytes 1540
  56.3 19.5 %all-to-all-start.2 = ((f32[32,32,128]{2,1,0:T(8,128)}), f32[32,32,128]{2,1,0:T(8,128)S(1)}, u32[]{:S(2)}, u32[]{:S(2)}) async-start(f32[32,32,128]{2,1,0:T(8,128)} %bitcast.40), calls=%async_computation.2 | async-start | bytes 1048576 | tf_op jit(solution)/shard_map/all_to_all | solution.py:162
  76.5 1.7 %copy-start.10 = (s32[64]{0:T(128)S(1)}, s32[64]{0:T(128)}, u32[]{:S(2)}) copy-start(s32[64]{0:T(128)} %get-tuple-element.5) | copy-start | bytes 772
  79.5 16.9 %copy-start.2 = (bf16[2,5120]{1,0:T(2,128)(2,1)S(1)}, bf16[2,5120]{1,0:T(2,128)(2,1)}, u32[]{:S(2)}) copy-start(bf16[2,5120]{1,0:T(2,128)(2,1)} %param.13) | copy-start | bytes 61444
